TPU v7x, 256 devices: a whole 4x4x8 slice. The times are simulated.
256 devices in a mesh: tok: 64 (over y, z, core), head: 4 (over x).
Axes of the slice: x: 4, y: 4, z: 8, core: 2. Of those that a mesh axis runs over, the one named last changes fastest.
Arguments:
- hidden: bfloat16 [2048, 2048], P('tok', 'head'), may hold values from -24 to 24
- attn_gain: float32 [2048], replicated, may hold values from 0.1 to 1.9
- w_query: bfloat16 [2048, 3072], P(None, 'head'), may hold values from -0.125 to 0.125
- w_latent: bfloat16 [2048, 576], P('head'), may hold values from -0.125 to 0.125
- w_key_up: bfloat16 [16, 128, 512], P('head'), may hold values from -0.5 to 0.5
- w_value_up: bfloat16 [16, 512, 128], P('head'), may hold values from -1 to 1
- w_out: bfloat16 [2048, 2048], P('head'), may hold values from -0.125 to 0.125
- latent_cache: bfloat16 [638976, 576], P(('tok', 'head')), may hold values from -6 to 6
- cache_lengths: int32 [2048], P('tok'), may hold values from 144 to 2048, as said below
- request_slot: int32 [2048], P('tok'), may hold values from 0 to 2047, as said below
- ffn_gain: float32 [2048], P('head'), may hold values from 0.1 to 1.9
- w_router: bfloat16 [2048, 64], P('head'), may hold values from -0.25 to 0.25
- routes: int32 [2048, 6], P('tok'), may hold values from 0 to 63, all different within a row; in each aligned block of 32 rows (0 to 31, 32 to 63, ...) at most 6 rows name the same one
- expert_gate: bfloat16 [64, 2048, 1408], P('tok', None, 'head'), may hold values from -0.125 to 0.125
- expert_up: bfloat16 [64, 2048, 1408], P('tok', None, 'head'), may hold values from -0.125 to 0.125
- expert_down: bfloat16 [64, 1408, 2048], P('tok', 'head'), may hold values from -0.15625 to 0.15625
Outputs:
- new_entry: bfloat16 [2048, 576], P('tok')
- attended: bfloat16 [2048, 2048], P('tok', 'head')
- expert_mix: bfloat16 [2048, 2048], P('tok', 'head')
Inputs may be any that keep to these rules, and one draw needn't show every extreme that they name: `request_slot`: a permutation of the 2048 slots; slot s lies on owner s // 32, so every owner holds 32 slots; the requests of one device name at most 1 slots of one owner, and every device reaches that bound. `cache_lengths`: the caches of an owner's slots lie end to end in slot order at the start of that owner's 9984 rows of latent_cache; they fill at most 9984 rows, and some owner fills all of them. `routes`: each row names 6 different experts; in the rows of one device no expert is named more than 6 times.
All inputs are finite; a program needn't handle non-finite values.
Results may differ from a plain program's by a relative error of at most 0.028.
Values may be sent and summed in bfloat16 or wider, within the bound.
No kernel may reach another device: no remote copies, remote signals or barrier semaphores. Data moves between devices by JAX's collectives and lax.ppermute only.
A program may use at most 128 MiB of HBM per device.

v0:
```python
import jax
import jax.numpy as jnp
from jax import lax
from jax.sharding import PartitionSpec as P

D = 2048
NOPE = 128
ROPE = 64
LATENT = 512
NORM_EPS = 1e-06


def rotate_pairs(values, places):
    halfway = values.shape[-1] // 2
    freqs = 10000.0 ** (-jnp.arange(halfway, dtype=jnp.float32) / halfway)
    angles = places.astype(jnp.float32).reshape(places.shape + (1,) * (values.ndim - 1)) * freqs
    cosine = jnp.cos(angles)
    sine = jnp.sin(angles)
    first_half = values[..., :halfway]
    second_half = values[..., halfway:]
    return jnp.concatenate(
        [first_half * cosine - second_half * sine, first_half * sine + second_half * cosine],
        axis=-1,
    )


def owner_attend(all_heads, owner_lengths, latent_cache, head_index, factor):
    slot_rows = all_heads.shape[0]
    total_heads = all_heads.shape[1]
    probe_width = all_heads.shape[2]
    key_rows = latent_cache.shape[0]
    starts = jnp.cumsum(owner_lengths) - owner_lengths
    places = head_index * key_rows + jnp.arange(key_rows, dtype=jnp.int32)
    inside = (places[None, :] >= starts[:, None]) & (
        places[None, :] < (starts + owner_lengths)[:, None]
    )
    scores = factor * jnp.einsum(
        "qc,pc->qp",
        all_heads.reshape(slot_rows * total_heads, probe_width),
        latent_cache,
        preferred_element_type=jnp.float32,
    )
    scores = scores.reshape(slot_rows, total_heads, key_rows)
    weights = jnp.where(inside[:, None, :], jnp.exp(scores), 0.0).astype(jnp.bfloat16)
    numerator = jnp.einsum(
        "khp,pl->khl", weights, latent_cache[:, :LATENT], preferred_element_type=jnp.float32
    )
    denominator = jnp.sum(weights.astype(jnp.float32), axis=2)
    return (numerator, denominator)


def head_sum_scatter(values, axis):
    groups = lax.axis_size("head")
    moved = lax.all_to_all(values, "head", split_axis=axis, concat_axis=0, tiled=True)
    moved = moved.reshape((groups, values.shape[0]) + moved.shape[1:])
    return jnp.sum(moved.astype(jnp.float32), axis=0)


def body(
    hidden,
    attn_gain,
    w_query,
    w_latent,
    w_key_up,
    w_value_up,
    w_out,
    latent_cache,
    cache_lengths,
    request_slot,
    ffn_gain,
    w_router,
    routes,
    expert_gate,
    expert_up,
    expert_down,
):
    local_rows = hidden.shape[0]
    quarter_width = hidden.shape[1]
    local_heads = w_key_up.shape[0]
    peer_count = lax.axis_size("tok")
    head_index = lax.axis_index("head")
    tok_index = lax.axis_index("tok")
    row_ids = jnp.arange(local_rows, dtype=jnp.int32)
    latent_width = w_latent.shape[1]
    head_count = lax.axis_size("head")
    gain_part = lax.dynamic_slice_in_dim(attn_gain, head_index * quarter_width, quarter_width, 0)
    raw_part = jnp.dot(
        (hidden.astype(jnp.float32) * gain_part).astype(jnp.bfloat16),
        w_latent,
        preferred_element_type=jnp.float32,
    )
    part_width = -(-latent_width // 128) * 128
    part_hi = lax.reduce_precision(raw_part, exponent_bits=8, mantissa_bits=7)
    rest = raw_part - part_hi
    part_mid = lax.reduce_precision(rest, exponent_bits=8, mantissa_bits=7)
    part_lo = rest - part_mid
    lane_pad = jnp.zeros((local_rows, part_width - latent_width), jnp.bfloat16)
    send_rows = jnp.concatenate(
        [
            hidden,
            part_hi.astype(jnp.bfloat16),
            lane_pad,
            part_mid.astype(jnp.bfloat16),
            lane_pad,
            part_lo.astype(jnp.bfloat16),
            lane_pad,
        ],
        axis=1,
    )
    got_rows = lax.all_gather(send_rows, "head", axis=0, tiled=False)
    hidden_groups = got_rows[:, :, :quarter_width].astype(jnp.float32)

    def part_piece(k):
        offset = quarter_width + k * part_width
        return got_rows[:, :, offset : offset + latent_width].astype(jnp.float32)

    part_sums = part_piece(0) + part_piece(1) + part_piece(2)
    inv_attn = lax.rsqrt(
        jnp.sum(hidden_groups * hidden_groups, axis=(0, 2))[:, None] / D + NORM_EPS
    )
    normed_groups = (
        hidden_groups * inv_attn[None] * attn_gain.reshape(head_count, 1, quarter_width)
    ).astype(jnp.bfloat16)
    compressed = jnp.sum(part_sums, axis=0) * inv_attn
    latent_new = compressed[:, :LATENT]
    latent_new = latent_new * lax.rsqrt(
        jnp.mean(latent_new * latent_new, axis=1, keepdims=True) + NORM_EPS
    )
    new_entry = jnp.concatenate(
        [latent_new, rotate_pairs(compressed[:, LATENT:], cache_lengths)], axis=1
    ).astype(jnp.bfloat16)
    queries = jnp.einsum(
        "gbf,gfq->bq",
        normed_groups,
        w_query.reshape(head_count, quarter_width, w_query.shape[1]),
        preferred_element_type=jnp.float32,
    ).astype(jnp.bfloat16)
    queries = queries.reshape(local_rows, local_heads, NOPE + ROPE)
    absorbed = jnp.einsum(
        "bhn,hnl->bhl", queries[:, :, :NOPE], w_key_up, preferred_element_type=jnp.float32
    ).astype(jnp.bfloat16)
    turned = rotate_pairs(queries[:, :, NOPE:].astype(jnp.float32), cache_lengths).astype(
        jnp.bfloat16
    )
    probes = jnp.concatenate([absorbed, turned], axis=2)
    factor = (NOPE + ROPE) ** (-0.5)
    owner_ids = jnp.arange(peer_count, dtype=jnp.int32)
    dest_owner = request_slot // local_rows
    goes_to = dest_owner[None, :] == owner_ids[:, None]
    sent_any = jnp.max(goes_to.astype(jnp.int32), axis=1)
    sent_row = jnp.sum(jnp.where(goes_to, row_ids[None, :], 0), axis=1)
    sent_slot = request_slot[sent_row]
    sent_len = cache_lengths[sent_row]
    code = (
        jnp.stack(
            [sent_any, sent_slot // 64, sent_slot % 64, sent_len // 64, sent_len % 64], axis=1
        )
        * sent_any[:, None]
    )
    code_row = jnp.zeros((peer_count, probes.shape[2]), jnp.float32)
    code_row = code_row.at[:, :5].set(code.astype(jnp.float32)).astype(jnp.bfloat16)
    packed = jnp.concatenate(
        [probes[sent_row], new_entry[sent_row][:, None, :], code_row[:, None, :]], axis=1
    )
    got_packed = lax.all_to_all(packed, "tok", 0, 0, tiled=True)
    got_code = got_packed[:, local_heads + 1, :5].astype(jnp.float32).astype(jnp.int32)
    got_slot = jnp.where(got_code[:, 0] > 0, got_code[:, 1] * 64 + got_code[:, 2], -1)
    got_len = got_code[:, 3] * 64 + got_code[:, 4]
    local_slot = got_slot - tok_index * local_rows
    slot_sel = local_slot[None, :] == row_ids[:, None]
    src_of_slot = jnp.sum(jnp.where(slot_sel, owner_ids[None, :], 0), axis=1)
    owner_probes = got_packed[src_of_slot, :local_heads]
    owner_lengths = got_len[src_of_slot]
    owner_new = got_packed[src_of_slot, local_heads]
    all_heads = lax.all_gather(owner_probes, "head", axis=1, tiled=True)
    numerator, denominator = owner_attend(
        all_heads, owner_lengths, latent_cache, head_index, factor
    )
    den_t = denominator.T
    den_hi = lax.reduce_precision(den_t, exponent_bits=8, mantissa_bits=7)
    den_rest = den_t - den_hi
    den_mid = lax.reduce_precision(den_rest, exponent_bits=8, mantissa_bits=7)
    den_lo = den_rest - den_mid
    den_row = jnp.zeros((3, denominator.shape[1], LATENT), jnp.float32)
    den_row = den_row.at[:, :, : denominator.shape[0]].set(jnp.stack([den_hi, den_mid, den_lo]))
    moved = lax.all_to_all(
        jnp.concatenate([numerator, den_row], axis=0).astype(jnp.bfloat16),
        "head",
        split_axis=1,
        concat_axis=0,
        tiled=True,
    ).astype(jnp.float32)
    moved = moved.reshape((head_count, local_rows + 3) + moved.shape[1:])
    joined = jnp.sum(moved[:, :local_rows], axis=0)
    den_parts = moved[:, local_rows:, :, :local_rows]
    group_den = jnp.sum(den_parts[:, 0] + den_parts[:, 1] + den_parts[:, 2], axis=0).T
    self_score = factor * jnp.einsum(
        "bhc,bc->bh", owner_probes, owner_new, preferred_element_type=jnp.float32
    )
    self_weight = jnp.exp(self_score).astype(jnp.bfloat16).astype(jnp.float32)
    total_num = joined[:local_rows] + self_weight[:, :, None] * owner_new[:, None, :LATENT].astype(
        jnp.float32
    )
    total_den = group_den + self_weight
    mixed_latent = (total_num / total_den[:, :, None]).astype(jnp.bfloat16)
    owner_out = jnp.einsum(
        "bhl,hld->bhd", mixed_latent, w_value_up, preferred_element_type=jnp.float32
    ).astype(jnp.bfloat16)
    owner_out = owner_out.reshape(local_rows, local_heads * NOPE)
    owner_out = jnp.concatenate(
        [owner_out, jnp.zeros((1, local_heads * NOPE), jnp.bfloat16)], axis=0
    )
    back_valid = (local_slot >= 0) & (local_slot < local_rows)
    back_row = jnp.where(back_valid, local_slot, local_rows)
    head_out = lax.all_to_all(owner_out[back_row], "tok", 0, 0, tiled=True)[dest_owner]
    head_out = head_out.reshape(local_rows, local_heads * NOPE)
    attn_piece = head_sum_scatter(
        jnp.dot(head_out, w_out, preferred_element_type=jnp.float32).astype(jnp.bfloat16), 1
    )
    attended = (hidden.astype(jnp.float32) + attn_piece).astype(jnp.bfloat16)
    attended_wide = attended.astype(jnp.float32)
    gained = (attended_wide * ffn_gain).astype(jnp.bfloat16)
    squares, logit_part = lax.psum(
        (
            jnp.sum(attended_wide * attended_wide, axis=1),
            jnp.dot(gained, w_router, preferred_element_type=jnp.float32),
        ),
        "head",
    )
    inv_ffn = lax.rsqrt(squares / D + NORM_EPS)
    logits = logit_part * inv_ffn[:, None]
    normed_ffn = (attended_wide * ffn_gain * inv_ffn[:, None]).astype(jnp.bfloat16)
    expert_count = w_router.shape[1]
    route_count = routes.shape[1]
    expert_ids = jnp.arange(expert_count, dtype=jnp.int32)
    named = routes[:, :, None] == expert_ids[None, None, :]
    picked = jnp.sum(jnp.where(named, logits[:, None, :], 0.0), axis=2)
    lifted = jnp.exp(picked)
    route_weight = lifted / jnp.sum(lifted, axis=1, keepdims=True)
    struck = jnp.max(named.astype(jnp.int32), axis=1)
    earlier_hits = jnp.cumsum(struck, axis=0) - struck
    capacity = min(local_rows, max(2, 2 * local_rows * route_count // expert_count))
    route_place = routes * capacity + jnp.take_along_axis(earlier_hits, routes, axis=1)
    slot_total = expert_count * capacity
    slot_ids = jnp.arange(slot_total, dtype=jnp.int32)
    filled = route_place[None, :, :] == slot_ids[:, None, None]
    source_token = jnp.sum(
        jnp.where(filled, row_ids[None, :, None], 0), axis=(1, 2)
    ) + local_rows * (1 - jnp.max(filled.astype(jnp.int32), axis=(1, 2)))
    padded_rows = jnp.concatenate(
        [normed_ffn, jnp.zeros((1, normed_ffn.shape[1]), jnp.bfloat16)], axis=0
    )
    arrived = lax.all_to_all(
        padded_rows[source_token].reshape(expert_count, capacity, quarter_width),
        "tok",
        split_axis=0,
        concat_axis=0,
        tiled=True,
    )
    expert_in = lax.all_to_all(
        jnp.broadcast_to(
            arrived.reshape(1, peer_count * capacity, quarter_width),
            (head_count, peer_count * capacity, quarter_width),
        ),
        "head",
        split_axis=0,
        concat_axis=2,
        tiled=True,
    ).reshape(peer_count * capacity, head_count * quarter_width)
    gate_value = jnp.dot(expert_in, expert_gate[0], preferred_element_type=jnp.float32)
    up_value = jnp.dot(expert_in, expert_up[0], preferred_element_type=jnp.float32)
    activity = (jax.nn.silu(gate_value) * up_value).astype(jnp.bfloat16)
    expert_share = head_sum_scatter(
        jnp.dot(activity, expert_down[0], preferred_element_type=jnp.float32).astype(jnp.bfloat16),
        1,
    ).astype(jnp.bfloat16)
    returned = lax.all_to_all(
        expert_share.reshape(peer_count, capacity, quarter_width),
        "tok",
        split_axis=0,
        concat_axis=0,
        tiled=True,
    )
    chosen_rows = returned.reshape(slot_total, quarter_width)[route_place]
    expert_mix = jnp.sum(route_weight[:, :, None] * chosen_rows.astype(jnp.float32), axis=1).astype(
        jnp.bfloat16
    )
    return (new_entry, attended, expert_mix)


def solution(mesh):
    in_specs = (
        P("tok", "head"),
        P(),
        P(None, "head"),
        P("head", None),
        P("head", None, None),
        P("head", None, None),
        P("head", None),
        P(("tok", "head"), None),
        P("tok"),
        P("tok"),
        P("head"),
        P("head", None),
        P("tok", None),
        P("tok", None, "head"),
        P("tok", None, "head"),
        P("tok", "head", None),
    )
    out_specs = (P("tok", None), P("tok", "head"), P("tok", "head"))
    return jax.shard_map(body, mesh=mesh, in_specs=in_specs, out_specs=out_specs, check_vma=False)
```

profile of v0, /device:TPU:1, one launch (start us, length us, event | category | flops | bytes accessed | tf_op | source)
XLA Modules:
  0.0 299.2 jit_solution(14646686963028986328)
XLA Ops:
  1.8 1.2 convert_element_type.154
  3.0 1.2 compare_select_fusion.5
  4.5 1.4 gather_fusion.3
  6.0 1.4 gather_fusion.2
  7.4 0.7 mul.256
  8.1 0.8 dynamic_slice.3
  8.9 1.4 fusion.44
  10.4 12.5 %all-gather = bf16[128,2432]{1,0:T(8,128)(2,1)S(1)} all-gather(bf16[32,2432]{1,0:T(8,128)(2,1)S(1)} %concatenate.36), channel_id=2, replica_groups=mesh['tok'=64,'head'=4] {'head'}, dimensions={0}, use_global_device_ids=true | all-gather | bytes 778240 | tf_op jit(solution)/shard_map/all_gather | solution.py:110
  26.6 1.0 broadcast_multiply_fusion
  27.8 1.4 multiply_cosine_fusion
  29.3 0.7 gather_fusion.1
  30.0 0.8 copy.305
  30.8 1.3 fusion.19
  32.1 0.8 subtract_convert_fusion
  33.1 1.6 gather_fusion
  34.7 2.5 pad_maximum_fusion
  37.1 14.2 %all-to-all-start = ((bf16[64,6,576]{2,1,0:T(8,128)(2,1)}), bf16[64,6,576]{2,1,0:T(8,128)(2,1)}, u32[]{:S(2)}, u32[]{:S(2)}) async-start(bf16[64,6,576]{2,1,0:T(8,128)(2,1)} %pad_maximum_fusion), calls=%async_computation | async-start | bytes 1310720 | tf_op jit(solution)/shard_map/all_to_all | solution.py:165
  51.7 1.6 gather_fusion.11
  54.1 0.7 convert_reduce_fusion.1
  54.8 16.5 %all-to-all-done = bf16[64,6,576]{2,1,0:T(8,128)(2,1)} async-done(((bf16[64,6,576]{2,1,0:T(8,128)(2,1)}), bf16[64,6,576]{2,1,0:T(8,128)(2,1)}, u32[]{:S(2)}, u32[]{:S(2)}) %all-to-all-start) | async-done | bytes 442400 | tf_op jit(solution)/shard_map/all_to_all | solution.py:165
  71.4 0.9 fusion.63
  73.7 1.9 copy.308
  75.7 1.8 gather_fusion.6
  77.4 2.1 gather_fusion.5
  79.6 12.1 %all_gather.11 = bf16[32,16,576]{2,0,1:T(8,128)(2,1)S(1)} all-gather(bf16[32,4,576]{2,0,1:T(8,128)(2,1)S(1)} %gather_fusion.5), channel_id=1, replica_groups=mesh['tok'=64,'head'=4] {'head'}, dimensions={1}, use_global_device_ids=true | all-gather | bytes 737280 | tf_op jit(solution)/shard_map/all_gather | solution.py:175
  92.4 1.4 copy.312
  93.9 4.5 %convert_reduce_fusion = (f32[512]{0:T(512)S(1)}, bf16[512,2496]{0,1:T(8,128)(2,1)}) fusion(pred[512,2496]{0,1:T(32,128)(4,1)S(1)} %copy.312, bf16[512,576]{1,0:T(8,128)(2,1)S(1)} %bitcast.144, bf16[2496,576]{0,1:T(8,128)(2,1)S(1)} %copy-done.12), kind=kOutput, calls=%fused_computation.13 | convolution fusion | flops 1478589952 | bytes 7301120 | tf_op jit(solution)/shard_map/qc,pc->qp/dot_general | solution.py:37
  98.6 4.4 %copy.310 = bf16[512,2496]{1,0:T(8,128)(2,1)} copy(bf16[512,2496]{0,1:T(8,128)(2,1)} %get-tuple-element.67) | data formatting | bytes 5111808 | tf_op jit(solution)/shard_map/exp | solution.py:44
  102.9 4.1 %fusion.10 = bf16[32,16,512]{2,1,0:T(8,128)(2,1)S(1)} fusion(bf16[2496,576]{0,1:T(8,128)(2,1)} %param.27, bf16[32,16,2496]{2,1,0:T(8,128)(2,1)} %bitcast.138, pred[32,2496]{1,0:T(8,128)(4,1)S(1)} %compare_and_fusion), kind=kOutput, calls=%fused_computation.29 | convolution fusion | flops 1310162944 | bytes 5847040 | tf_op jit(solution)/shard_map/khp,pl->khl/dot_general | solution.py:45
  107.1 1.2 copy.314
  108.3 4.2 %all-to-all-start.1 = ((bf16[35,16,512]{2,0,1:T(8,128)(2,1)}), bf16[35,16,512]{2,0,1:T(8,128)(2,1)}, u32[]{:S(2)}, u32[]{:S(2)}) async-start(bf16[35,16,512]{2,0,1:T(8,128)(2,1)} %copy.314), calls=%async_computation.1 | async-start | bytes 1310720 | tf_op jit(solution)/shard_map/all_to_all | solution.py:186
  114.0 6.6 %all-to-all-done.1 = bf16[35,16,512]{2,0,1:T(8,128)(2,1)} async-done(((bf16[35,16,512]{2,0,1:T(8,128)(2,1)}), bf16[35,16,512]{2,0,1:T(8,128)(2,1)}, u32[]{:S(2)}, u32[]{:S(2)}) %all-to-all-start.1) | async-done | bytes 573472 | tf_op jit(solution)/shard_map/all_to_all | solution.py:186
  120.6 1.4 copy.358
  123.0 0.8 copy.318
  123.9 1.2 fusion.21
  125.2 0.8 gather_fusion.7
  127.8 9.3 %all-to-all-start.2 = ((bf16[64,2,256]{2,1,0:T(2,128)(2,1)}), bf16[64,2,256]{2,1,0:T(2,128)(2,1)S(1)}, u32[]{:S(2)}, u32[]{:S(2)}) async-start(bf16[64,2,256]{2,1,0:T(2,128)(2,1)} %reshape.670), calls=%async_computation.2 | async-start | bytes 131072 | tf_op jit(solution)/shard_map/all_to_all | solution.py:215
  137.9 9.1 %all-to-all-done.2 = bf16[64,2,256]{2,1,0:T(2,128)(2,1)S(1)} async-done(((bf16[64,2,256]{2,1,0:T(2,128)(2,1)}), bf16[64,2,256]{2,1,0:T(2,128)(2,1)S(1)}, u32[]{:S(2)}, u32[]{:S(2)}) %all-to-all-start.2) | async-done | bytes 65568 | tf_op jit(solution)/shard_map/all_to_all | solution.py:215
  147.7 2.1 convolution_convert_fusion.1
  150.4 3.3 %all-to-all-start.3 = ((bf16[32,4,512]{2,0,1:T(8,128)(2,1)}), bf16[32,4,512]{2,0,1:T(8,128)(2,1)S(1)}, u32[]{:S(2)}, u32[]{:S(2)}) async-start(bf16[32,4,512]{2,0,1:T(8,128)(2,1)} %bitcast.127), calls=%async_computation.3 | async-start | bytes 262144 | tf_op jit(solution)/shard_map/all_to_all | solution.py:54
  153.7 4.8 %all-to-all-done.3 = bf16[32,4,512]{2,0,1:T(8,128)(2,1)S(1)} async-done(((bf16[32,4,512]{2,0,1:T(8,128)(2,1)}), bf16[32,4,512]{2,0,1:T(8,128)(2,1)S(1)}, u32[]{:S(2)}, u32[]{:S(2)}) %all-to-all-start.3) | async-done | bytes 131104 | tf_op jit(solution)/shard_map/all_to_all | solution.py:54
  158.8 12.5 %all-reduce.6 = (f32[32]{0:T(128)S(1)}, f32[32,64]{1,0:T(8,128)}) all-reduce(f32[32]{0:T(128)S(1)} %get-tuple-element.37, f32[32,64]{1,0:T(8,128)S(1)} %fusion.56), channel_id=1, replica_groups=mesh['tok'=64,'head'=4] {'head'}, use_global_device_ids=true, to_apply=%region_14.15 | all-reduce | flops 2080 | bytes 16640 | tf_op jit(solution)/shard_map/psum | solution.py:223
  171.5 2.6 gather_fusion.9
  174.0 1.9 reshape.555
  175.9 27.4 %all_to_all.77 = bf16[64,6,512]{2,1,0:T(8,128)(2,1)} all-to-all(bf16[64,6,512]{2,1,0:T(8,128)(2,1)} %reshape.555), channel_id=1, replica_groups=mesh['tok'=64,'head'=4] {'tok'}, dimensions={0} | all-to-all | bytes 786432 | tf_op jit(solution)/shard_map/all_to_all | solution.py:253
  203.3 1.2 broadcast_in_dim.156
  204.5 0.9 copy.329
  205.4 1.1 broadcast_in_dim.157
  206.5 23.0 %all_to_all.78 = bf16[4,384,512]{1,2,0:T(8,128)(2,1)S(1)} all-to-all(bf16[4,384,512]{1,2,0:T(8,128)(2,1)S(1)} %broadcast_in_dim.157), channel_id=1, replica_groups=mesh['tok'=64,'head'=4] {'head'}, dimensions={0} | all-to-all | bytes 3145728 | tf_op jit(solution)/shard_map/all_to_all | solution.py:260
  229.6 1.1 copy-done.2
  230.7 1.7 fusion.8
  232.4 5.5 %convolution_convert_fusion = bf16[384,2048]{1,0:T(8,128)(2,1)} fusion(bf16[1,352,2048]{2,1,0:T(8,128)(2,1)} %param.35, bf16[384,2048]{0,1:T(8,128)(2,1)} %bitcast.141, bf16[1,2048,352]{1,2,0:T(8,128)(2,1)} %param.34, f32[384,352]{0,1:T(8,128)} %fusion.8), kind=kOutput, calls=%fused_computation.16 | convolution fusion | flops 1108893696 | bytes 6569984 | tf_op jit(solution)/shard_map/dot_general | solution.py:274
  237.9 2.7 copy.357
  240.6 4.5 %all-to-all-start.6 = ((bf16[384,4,512]{2,0,1:T(8,128)(2,1)}), bf16[384,4,512]{2,0,1:T(8,128)(2,1)}, u32[]{:S(2)}, u32[]{:S(2)}) async-start(bf16[384,4,512]{2,0,1:T(8,128)(2,1)} %bitcast.131), calls=%async_computation.6 | async-start | bytes 3145728 | tf_op jit(solution)/shard_map/all_to_all | solution.py:54
  245.2 19.5 %all-to-all-done.6 = bf16[384,4,512]{2,0,1:T(8,128)(2,1)} async-done(((bf16[384,4,512]{2,0,1:T(8,128)(2,1)}), bf16[384,4,512]{2,0,1:T(8,128)(2,1)}, u32[]{:S(2)}, u32[]{:S(2)}) %all-to-all-start.6) | async-done | bytes 1572896 | tf_op jit(solution)/shard_map/all_to_all | solution.py:54
  264.7 1.8 reduce_sum.160
  266.5 0.9 reshape.557
  267.4 8.1 %all-to-all-start.7 = ((bf16[64,6,512]{2,1,0:T(8,128)(2,1)}), bf16[64,6,512]{2,1,0:T(8,128)(2,1)}, u32[]{:S(2)}, u32[]{:S(2)}) async-start(bf16[64,6,512]{2,1,0:T(8,128)(2,1)} %reshape.557), calls=%async_computation.7 | async-start | bytes 1048576 | tf_op jit(solution)/shard_map/all_to_all | solution.py:277
  275.5 0.8 broadcast_multiply_fusion.1
  277.2 15.5 %all-to-all-done.7 = bf16[64,6,512]{2,1,0:T(8,128)(2,1)} async-done(((bf16[64,6,512]{2,1,0:T(8,128)(2,1)}), bf16[64,6,512]{2,1,0:T(8,128)(2,1)}, u32[]{:S(2)}, u32[]{:S(2)}) %all-to-all-start.7) | async-done | bytes 393248 | tf_op jit(solution)/shard_map/all_to_all | solution.py:277
  292.7 1.2 reshape.558
  293.9 1.7 gather_fusion.10
  295.6 1.8 reshape.654
  297.3 1.9 multiply_reduce_fusion
  (123 shorter events, 17.2 us)
Async XLA Ops:
  0.6 23.1 %copy-start = (bf16[2048,768]{1,0:T(8,128)(2,1)S(1)}, bf16[2048,768]{1,0:T(8,128)(2,1)}, u32[]{:S(2)}) copy-start(bf16[2048,768]{1,0:T(8,128)(2,1)} %param.22) | copy-start | bytes 9437188
  0.6 9.6 %copy-start.4 = (bf16[32,512]{1,0:T(8,128)(2,1)S(1)}, bf16[32,512]{1,0:T(8,128)(2,1)}, u32[]{:S(2)}) copy-start(bf16[32,512]{1,0:T(8,128)(2,1)} %param.20) | copy-start | bytes 98308
  23.7 4.1 %copy-start.11 = (f32[32]{0:T(128)S(1)}, f32[32]{0:T(128)}, u32[]{:S(2)}) copy-start(f32[32]{0:T(128)} %multiply_power_fusion) | copy-start | bytes 388
  29.3 5.4 %copy-start.1 = (bf16[32,576]{1,0:T(8,128)(2,1)}, bf16[32,576]{1,0:T(8,128)(2,1)S(1)}, u32[]{:S(2)}) copy-start(bf16[32,576]{1,0:T(8,128)(2,1)S(1)} %pad_maximum_fusion.3) | copy-start | bytes 110596
  33.1 18.2 %copy-start.7 = (s32[32,6]{0,1:T(8,128)S(1)}, s32[32,6]{0,1:T(8,128)}, u32[]{:S(2)}) copy-start(s32[32,6]{0,1:T(8,128)} %param.32) | copy-start | bytes 2308
  37.1 34.2 %all-to-all-start = ((bf16[64,6,576]{2,1,0:T(8,128)(2,1)}), bf16[64,6,576]{2,1,0:T(8,128)(2,1)}, u32[]{:S(2)}, u32[]{:S(2)}) async-start(bf16[64,6,576]{2,1,0:T(8,128)(2,1)} %pad_maximum_fusion), calls=%async_computation | async-start | bytes 1310720 | tf_op jit(solution)/shard_map/all_to_all | solution.py:165
  92.0 1.8 copy-start.12
  108.3 12.4 %all-to-all-start.1 = ((bf16[35,16,512]{2,0,1:T(8,128)(2,1)}), bf16[35,16,512]{2,0,1:T(8,128)(2,1)}, u32[]{:S(2)}, u32[]{:S(2)}) async-start(bf16[35,16,512]{2,0,1:T(8,128)(2,1)} %copy.314), calls=%async_computation.1 | async-start | bytes 1310720 | tf_op jit(solution)/shard_map/all_to_all | solution.py:186
  114.0 8.3 %copy-start.10 = (f32[32,1,4]{0,2,1:T(4,128)S(1)}, f32[32,1,4]{0,2,1:T(4,128)}, u32[]{:S(2)}) copy-start(f32[32,1,4]{0,2,1:T(4,128)} %copy.333) | copy-start | bytes 1540
  122.1 15.1 %copy-start.9 = (s32[384]{0:T(512)S(1)}, s32[384]{0:T(512)}, u32[]{:S(2)}) copy-start(s32[384]{0:T(512)} %get-tuple-element.30) | copy-start | bytes 4612
  127.8 19.1 %all-to-all-start.2 = ((bf16[64,2,256]{2,1,0:T(2,128)(2,1)}), bf16[64,2,256]{2,1,0:T(2,128)(2,1)S(1)}, u32[]{:S(2)}, u32[]{:S(2)}) async-start(bf16[64,2,256]{2,1,0:T(2,128)(2,1)} %reshape.670), calls=%async_computation.2 | async-start | bytes 131072 | tf_op jit(solution)/shard_map/all_to_all | solution.py:215
  147.6 11.1 %copy-start.5 = (bf16[512,64]{0,1:T(8,128)(2,1)S(1)}, bf16[512,64]{0,1:T(8,128)(2,1)}, u32[]{:S(2)}) copy-start(bf16[512,64]{0,1:T(8,128)(2,1)} %param.31) | copy-start | bytes 196612
  147.6 11.0 %copy-start.8 = (f32[512]{0:T(512)S(1)}, f32[512]{0:T(512)}, u32[]{:S(2)}) copy-start(f32[512]{0:T(512)} %param.30) | copy-start | bytes 6148
  150.4 8.1 %all-to-all-start.3 = ((bf16[32,4,512]{2,0,1:T(8,128)(2,1)}), bf16[32,4,512]{2,0,1:T(8,128)(2,1)S(1)}, u32[]{:S(2)}, u32[]{:S(2)}) async-start(bf16[32,4,512]{2,0,1:T(8,128)(2,1)} %bitcast.127), calls=%async_computation.3 | async-start | bytes 262144 | tf_op jit(solution)/shard_map/all_to_all | solution.py:54
  158.7 12.7 %copy-start.3 = (bf16[32,512]{1,0:T(8,128)(2,1)}, bf16[32,512]{1,0:T(8,128)(2,1)S(1)}, u32[]{:S(2)}) copy-start(bf16[32,512]{1,0:T(8,128)(2,1)S(1)} %get-tuple-element.38) | copy-start | bytes 98308
  206.5 24.2 %copy-start.13 = (bf16[1,2048,352]{1,2,0:T(8,128)(2,1)S(1)}, bf16[1,2048,352]{1,2,0:T(8,128)(2,1)}, u32[]{:S(2)}) copy-start(bf16[1,2048,352]{1,2,0:T(8,128)(2,1)} %param.33) | copy-start | bytes 4325380
  229.6 1.1 copy-start.2
  240.6 4.5 %copy-start.6 = (s32[32,6]{1,0:T(8,128)S(1)}, s32[32,6]{1,0:T(8,128)}, u32[]{:S(2)}) copy-start(s32[32,6]{1,0:T(8,128)} %get-tuple-element.35) | copy-start | bytes 2308
  240.6 24.1 %all-to-all-start.6 = ((bf16[384,4,512]{2,0,1:T(8,128)(2,1)}), bf16[384,4,512]{2,0,1:T(8,128)(2,1)}, u32[]{:S(2)}, u32[]{:S(2)}) async-start(bf16[384,4,512]{2,0,1:T(8,128)(2,1)} %bitcast.131), calls=%async_computation.6 | async-start | bytes 3145728 | tf_op jit(solution)/shard_map/all_to_all | solution.py:54
  267.4 25.3 %all-to-all-start.7 = ((bf16[64,6,512]{2,1,0:T(8,128)(2,1)}), bf16[64,6,512]{2,1,0:T(8,128)(2,1)}, u32[]{:S(2)}, u32[]{:S(2)}) async-start(bf16[64,6,512]{2,1,0:T(8,128)(2,1)} %reshape.557), calls=%async_computation.7 | async-start | bytes 1048576 | tf_op jit(solution)/shard_map/all_to_all | solution.py:277
where the time goes:
time: 301 us; the launch traced here: 299 us
  blocking collectives  87.5 us (29%)
  waiting for transfers between devices  72 us (24%)
  local copies, waits for them, and re-layouts  49.7 us (17%)
  starting transfers between devices  43.5 us (14%)
  matrix products  22.8 us (8%)
  other arithmetic  22.5 us (7%)
    all_to_all x1, blocking collectives, body(): lax.all_to_all(padded_rows[source_token].reshape(expert_count, capacity,...  27.4 us
    all_to_all x2, waiting for transfers between devices, head_sum_scatter(): lax.all_to_all(values, 'head', split_axis=axis, concat_axis=0, tiled=True)  24.3 us
    all_to_all x1, blocking collectives, body(): lax.all_to_all(jnp.broadcast_to(arrived.reshape(1, peer_count * capacity,...  23 us
    all_to_all x1, waiting for transfers between devices, body(): got_packed = lax.all_to_all(packed, 'tok', 0, 0, tiled=True)  16.5 us
    all_to_all x1, waiting for transfers between devices, body(): lax.all_to_all(expert_share.reshape(peer_count, capacity, quarter_width),...  15.5 us
    all_to_all x1, starting transfers between devices, body(): got_packed = lax.all_to_all(packed, 'tok', 0, 0, tiled=True)  14.2 us
    psum x1, blocking collectives, body(): lax.psum((jnp.sum(attended_wide * attended_wide, axis=1), jnp.dot(gained,...  12.5 us
    all_gather x1, blocking collectives, body(): got_rows = lax.all_gather(send_rows, 'head', axis=0, tiled=False)  12.5 us
  transfers between devices with their start and end apart: 6, of which 6 were waited for; matrix products, arithmetic and copies ran while one was open for 3% of the time, Pallas kernels for 0%

commit v1 on v0

--- a/solution.py
+++ b/solution.py
@@ -172,7 +172,9 @@
     owner_probes = got_packed[src_of_slot, :local_heads]
     owner_lengths = got_len[src_of_slot]
     owner_new = got_packed[src_of_slot, local_heads]
-    all_heads = lax.all_gather(owner_probes, "head", axis=1, tiled=True)
+    all_heads = jnp.concatenate(
+        lax.all_to_all(jnp.stack([owner_probes] * lax.axis_size("head")), "head", 0, 0), axis=1
+    )
     numerator, denominator = owner_attend(
         all_heads, owner_lengths, latent_cache, head_index, factor
     )

time: 301 us -> 311 us (1.033)
  blocking collectives: 87.5 us -> 75.2 us
  waiting for transfers between devices: 72 us -> 80.5 us
  local copies, waits for them, and re-layouts: 49.7 us -> 56 us
    all_gather x1 -> x0, blocking collectives: 12.1 us -> none  [body(): all_heads = lax.all_gather(owner_probes, 'head', axis=1, tiled=True)]
    all_to_all x0 -> x1, waiting for transfers between devices: none -> 7.48 us  [body(): lax.all_to_all(jnp.stack([owner_probes] * lax.axis_size('head')), 'head',...]
    all_to_all x0 -> x1, starting transfers between devices: none -> 4.34 us  [body(): lax.all_to_all(jnp.stack([owner_probes] * lax.axis_size('head')), 'head',...]
    another operation x1 -> x3, local copies, waits for them, and re-layouts: 0.09 us -> 3.34 us  [the longest x1 2.24 us: owner_attend(): all_heads.reshape(slot_rows * total_heads, probe_width)]
  transfers between devices with their start and end apart: 6 -> 7, of which waited for: 6 -> 7; matrix products, arithmetic and copies ran while one was open for 3% -> 4% of each run, Pallas kernels for 0% -> 0%
where the time goes in v1:
time: 311 us; the launch traced here: 309 us
  waiting for transfers between devices  80.5 us (26%)
  blocking collectives  75.2 us (24%)
  local copies, waits for them, and re-layouts  56 us (18%)
  starting transfers between devices  46.4 us (15%)
  matrix products  25.1 us (8%)
  other arithmetic  24.2 us (8%)
    all_to_all x1, blocking collectives, body(): lax.all_to_all(padded_rows[source_token].reshape(expert_count, capacity,...  27.4 us
    all_to_all x2, waiting for transfers between devices, head_sum_scatter(): lax.all_to_all(values, 'head', split_axis=axis, concat_axis=0, tiled=True)  24.3 us
    all_to_all x1, blocking collectives, body(): lax.all_to_all(jnp.broadcast_to(arrived.reshape(1, peer_count * capacity,...  23 us
    all_to_all x1, waiting for transfers between devices, body(): got_packed = lax.all_to_all(packed, 'tok', 0, 0, tiled=True)  15.9 us
    all_to_all x1, waiting for transfers between devices, body(): lax.all_to_all(expert_share.reshape(peer_count, capacity, quarter_width),...  15.5 us
    all_to_all x1, starting transfers between devices, body(): got_packed = lax.all_to_all(packed, 'tok', 0, 0, tiled=True)  14.2 us
    all_gather x1, blocking collectives, body(): got_rows = lax.all_gather(send_rows, 'head', axis=0, tiled=False)  12.5 us
    psum x1, blocking collectives, body(): lax.psum((jnp.sum(attended_wide * attended_wide, axis=1), jnp.dot(gained,...  12.3 us
  transfers between devices with their start and end apart: 7, of which 7 were waited for; matrix products, arithmetic and copies ran while one was open for 4% of the time, Pallas kernels for 0%

profile of v1, /device:TPU:1, one launch (start us, length us, event | category | flops | bytes accessed | tf_op | source)
XLA Modules:
  0.0 308.6 jit_solution(17066194232825080103)
XLA Ops:
  1.8 1.2 convert_element_type.154
  3.0 1.2 compare_select_fusion.5
  4.5 1.4 gather_fusion.3
  6.0 1.4 gather_fusion.2
  8.9 1.4 fusion.42
  10.4 12.5 %all-gather = bf16[128,2432]{1,0:T(8,128)(2,1)S(1)} all-gather(bf16[32,2432]{1,0:T(8,128)(2,1)S(1)} %concatenate.36), channel_id=2, replica_groups=mesh['tok'=64,'head'=4] {'head'}, dimensions={0}, use_global_device_ids=true | all-gather | bytes 778240 | tf_op jit(solution)/shard_map/all_gather | solution.py:110
  26.6 1.0 broadcast_multiply_fusion
  27.8 1.4 multiply_cosine_fusion
  30.0 0.8 copy.310
  30.8 1.3 fusion.19
  32.1 0.8 subtract_convert_fusion
  33.1 1.6 gather_fusion
  34.7 2.5 pad_maximum_fusion
  37.1 14.2 %all-to-all-start = ((bf16[64,6,576]{2,1,0:T(8,128)(2,1)}), bf16[64,6,576]{2,1,0:T(8,128)(2,1)}, u32[]{:S(2)}, u32[]{:S(2)}) async-start(bf16[64,6,576]{2,1,0:T(8,128)(2,1)} %pad_maximum_fusion), calls=%async_computation | async-start | bytes 1310720 | tf_op jit(solution)/shard_map/all_to_all | solution.py:165
  51.7 1.6 gather_fusion.11
  55.4 15.9 %all-to-all-done = bf16[64,6,576]{2,1,0:T(8,128)(2,1)} async-done(((bf16[64,6,576]{2,1,0:T(8,128)(2,1)}), bf16[64,6,576]{2,1,0:T(8,128)(2,1)}, u32[]{:S(2)}, u32[]{:S(2)}) %all-to-all-start) | async-done | bytes 442400 | tf_op jit(solution)/shard_map/all_to_all | solution.py:165
  71.3 0.9 fusion.62
  74.8 1.9 copy.313
  76.8 1.8 gather_fusion.6
  78.5 2.1 gather_fusion.5
  80.8 1.0 stack.35
  81.8 4.3 %all-to-all-start.1 = ((bf16[4,32,4,576]{3,2,1,0:T(4,128)(2,1)}), bf16[4,32,4,576]{3,2,1,0:T(4,128)(2,1)}, u32[]{:S(2)}, u32[]{:S(2)}) async-start(bf16[4,32,4,576]{3,2,1,0:T(4,128)(2,1)} %stack.35), calls=%async_computation.1 | async-start | bytes 1310720 | tf_op jit(solution)/shard_map/all_to_all | solution.py:176
  86.7 2.5 copy.318
  89.1 7.5 %all-to-all-done.1 = bf16[4,32,4,576]{3,2,1,0:T(4,128)(2,1)} async-done(((bf16[4,32,4,576]{3,2,1,0:T(4,128)(2,1)}), bf16[4,32,4,576]{3,2,1,0:T(4,128)(2,1)}, u32[]{:S(2)}, u32[]{:S(2)}) %all-to-all-start.1) | async-done | bytes 589856 | tf_op jit(solution)/shard_map/all_to_all | solution.py:176
  96.6 2.1 copy.315
  98.8 2.2 reshape_reshape.3
  101.0 6.8 %convert_reduce_fusion = (f32[512]{0:T(512)S(1)}, bf16[512,2496]{0,1:T(8,128)(2,1)}) fusion(pred[512,2496]{0,1:T(32,128)(4,1)} %copy.318, bf16[512,576]{1,0:T(8,128)(2,1)} %reshape_reshape.3, bf16[2496,576]{0,1:T(8,128)(2,1)} %param.27), kind=kOutput, calls=%fused_computation.13 | convolution fusion | flops 1478589952 | bytes 7301120 | tf_op jit(solution)/shard_map/qc,pc->qp/dot_general | solution.py:37
  108.0 4.4 %copy.316 = bf16[512,2496]{1,0:T(8,128)(2,1)} copy(bf16[512,2496]{0,1:T(8,128)(2,1)} %get-tuple-element.67) | data formatting | bytes 5111808 | tf_op jit(solution)/shard_map/exp | solution.py:44
  112.4 4.1 %fusion.10 = bf16[32,16,512]{2,1,0:T(8,128)(2,1)S(1)} fusion(bf16[2496,576]{0,1:T(8,128)(2,1)} %param.27, bf16[32,16,2496]{2,1,0:T(8,128)(2,1)} %bitcast.139, pred[32,2496]{1,0:T(8,128)(4,1)S(1)} %compare_and_fusion), kind=kOutput, calls=%fused_computation.29 | convolution fusion | flops 1310162944 | bytes 5847040 | tf_op jit(solution)/shard_map/khp,pl->khl/dot_general | solution.py:45
  116.6 1.2 copy.320
  117.8 4.2 %all-to-all-start.2 = ((bf16[35,16,512]{2,0,1:T(8,128)(2,1)}), bf16[35,16,512]{2,0,1:T(8,128)(2,1)}, u32[]{:S(2)}, u32[]{:S(2)}) async-start(bf16[35,16,512]{2,0,1:T(8,128)(2,1)} %copy.320), calls=%async_computation.2 | async-start | bytes 1310720 | tf_op jit(solution)/shard_map/all_to_all | solution.py:188
  123.5 8.2 %all-to-all-done.2 = bf16[35,16,512]{2,0,1:T(8,128)(2,1)} async-done(((bf16[35,16,512]{2,0,1:T(8,128)(2,1)}), bf16[35,16,512]{2,0,1:T(8,128)(2,1)}, u32[]{:S(2)}, u32[]{:S(2)}) %all-to-all-start.2) | async-done | bytes 573472 | tf_op jit(solution)/shard_map/all_to_all | solution.py:188
  131.7 1.4 copy.361
  134.0 0.8 copy.324
  134.9 1.2 fusion.21
  136.2 0.8 gather_fusion.7
  138.9 7.8 %all-to-all-start.3 = ((bf16[64,2,256]{2,1,0:T(2,128)(2,1)}), bf16[64,2,256]{2,1,0:T(2,128)(2,1)S(1)}, u32[]{:S(2)}, u32[]{:S(2)}) async-start(bf16[64,2,256]{2,1,0:T(2,128)(2,1)} %reshape.672), calls=%async_computation.3 | async-start | bytes 131072 | tf_op jit(solution)/shard_map/all_to_all | solution.py:217
  147.4 9.1 %all-to-all-done.3 = bf16[64,2,256]{2,1,0:T(2,128)(2,1)S(1)} async-done(((bf16[64,2,256]{2,1,0:T(2,128)(2,1)}), bf16[64,2,256]{2,1,0:T(2,128)(2,1)S(1)}, u32[]{:S(2)}, u32[]{:S(2)}) %all-to-all-start.3) | async-done | bytes 65568 | tf_op jit(solution)/shard_map/all_to_all | solution.py:217
  157.2 2.1 convolution_convert_fusion.1
  160.0 3.3 %all-to-all-start.4 = ((bf16[32,4,512]{2,0,1:T(8,128)(2,1)}), bf16[32,4,512]{2,0,1:T(8,128)(2,1)S(1)}, u32[]{:S(2)}, u32[]{:S(2)}) async-start(bf16[32,4,512]{2,0,1:T(8,128)(2,1)} %bitcast.128), calls=%async_computation.4 | async-start | bytes 262144 | tf_op jit(solution)/shard_map/all_to_all | solution.py:54
  163.3 4.8 %all-to-all-done.4 = bf16[32,4,512]{2,0,1:T(8,128)(2,1)S(1)} async-done(((bf16[32,4,512]{2,0,1:T(8,128)(2,1)}), bf16[32,4,512]{2,0,1:T(8,128)(2,1)S(1)}, u32[]{:S(2)}, u32[]{:S(2)}) %all-to-all-start.4) | async-done | bytes 131104 | tf_op jit(solution)/shard_map/all_to_all | solution.py:54
  168.4 12.3 %all-reduce.6 = (f32[32]{0:T(128)S(1)}, f32[32,64]{1,0:T(8,128)}) all-reduce(f32[32]{0:T(128)S(1)} %get-tuple-element.37, f32[32,64]{1,0:T(8,128)S(1)} %fusion.55), channel_id=1, replica_groups=mesh['tok'=64,'head'=4] {'head'}, use_global_device_ids=true, to_apply=%region_14.15 | all-reduce | flops 2080 | bytes 16640 | tf_op jit(solution)/shard_map/psum | solution.py:225
  180.8 2.6 gather_fusion.9
  183.3 1.9 reshape.557
  185.3 27.4 %all_to_all.82 = bf16[64,6,512]{2,1,0:T(8,128)(2,1)} all-to-all(bf16[64,6,512]{2,1,0:T(8,128)(2,1)} %reshape.557), channel_id=1, replica_groups=mesh['tok'=64,'head'=4] {'tok'}, dimensions={0} | all-to-all | bytes 786432 | tf_op jit(solution)/shard_map/all_to_all | solution.py:255
  212.7 1.2 broadcast_in_dim.156
  213.9 0.9 copy.335
  214.8 1.1 broadcast_in_dim.157
  215.9 23.0 %all_to_all.83 = bf16[4,384,512]{1,2,0:T(8,128)(2,1)S(1)} all-to-all(bf16[4,384,512]{1,2,0:T(8,128)(2,1)S(1)} %broadcast_in_dim.157), channel_id=1, replica_groups=mesh['tok'=64,'head'=4] {'head'}, dimensions={0} | all-to-all | bytes 3145728 | tf_op jit(solution)/shard_map/all_to_all | solution.py:262
  239.0 1.1 copy-done.2
  240.1 1.7 fusion.8
  241.8 5.5 %convolution_convert_fusion = bf16[384,2048]{1,0:T(8,128)(2,1)} fusion(bf16[1,352,2048]{2,1,0:T(8,128)(2,1)} %param.35, bf16[384,2048]{0,1:T(8,128)(2,1)} %bitcast.142, bf16[1,2048,352]{1,2,0:T(8,128)(2,1)} %param.34, f32[384,352]{0,1:T(8,128)} %fusion.8), kind=kOutput, calls=%fused_computation.16 | convolution fusion | flops 1108893696 | bytes 6569984 | tf_op jit(solution)/shard_map/dot_general | solution.py:276
  247.3 2.7 copy.360
  250.0 4.5 %all-to-all-start.7 = ((bf16[384,4,512]{2,0,1:T(8,128)(2,1)}), bf16[384,4,512]{2,0,1:T(8,128)(2,1)}, u32[]{:S(2)}, u32[]{:S(2)}) async-start(bf16[384,4,512]{2,0,1:T(8,128)(2,1)} %bitcast.132), calls=%async_computation.7 | async-start | bytes 3145728 | tf_op jit(solution)/shard_map/all_to_all | solution.py:54
  254.6 19.5 %all-to-all-done.7 = bf16[384,4,512]{2,0,1:T(8,128)(2,1)} async-done(((bf16[384,4,512]{2,0,1:T(8,128)(2,1)}), bf16[384,4,512]{2,0,1:T(8,128)(2,1)}, u32[]{:S(2)}, u32[]{:S(2)}) %all-to-all-start.7) | async-done | bytes 1572896 | tf_op jit(solution)/shard_map/all_to_all | solution.py:54
  274.1 1.8 reduce_sum.160
  275.9 0.9 reshape.559
  276.8 8.1 %all-to-all-start.8 = ((bf16[64,6,512]{2,1,0:T(8,128)(2,1)}), bf16[64,6,512]{2,1,0:T(8,128)(2,1)}, u32[]{:S(2)}, u32[]{:S(2)}) async-start(bf16[64,6,512]{2,1,0:T(8,128)(2,1)} %reshape.559), calls=%async_computation.8 | async-start | bytes 1048576 | tf_op jit(solution)/shard_map/all_to_all | solution.py:279
  284.9 0.8 broadcast_multiply_fusion.1
  286.6 15.5 %all-to-all-done.8 = bf16[64,6,512]{2,1,0:T(8,128)(2,1)} async-done(((bf16[64,6,512]{2,1,0:T(8,128)(2,1)}), bf16[64,6,512]{2,1,0:T(8,128)(2,1)}, u32[]{:S(2)}, u32[]{:S(2)}) %all-to-all-start.8) | async-done | bytes 393248 | tf_op jit(solution)/shard_map/all_to_all | solution.py:279
  302.1 1.2 reshape.560
  303.3 1.7 gather_fusion.10
  305.0 1.8 reshape.656
  306.7 1.9 multiply_reduce_fusion
  (135 shorter events, 21.7 us)
Async XLA Ops:
  0.6 23.1 %copy-start = (bf16[2048,768]{1,0:T(8,128)(2,1)S(1)}, bf16[2048,768]{1,0:T(8,128)(2,1)}, u32[]{:S(2)}) copy-start(bf16[2048,768]{1,0:T(8,128)(2,1)} %param.22) | copy-start | bytes 9437188
  0.6 9.6 %copy-start.4 = (bf16[32,512]{1,0:T(8,128)(2,1)S(1)}, bf16[32,512]{1,0:T(8,128)(2,1)}, u32[]{:S(2)}) copy-start(bf16[32,512]{1,0:T(8,128)(2,1)} %param.20) | copy-start | bytes 98308
  23.7 4.1 %copy-start.16 = (f32[32]{0:T(128)S(1)}, f32[32]{0:T(128)}, u32[]{:S(2)}) copy-start(f32[32]{0:T(128)} %multiply_power_fusion) | copy-start | bytes 388
  29.3 5.3 %copy-start.1 = (bf16[32,576]{1,0:T(8,128)(2,1)}, bf16[32,576]{1,0:T(8,128)(2,1)S(1)}, u32[]{:S(2)}) copy-start(bf16[32,576]{1,0:T(8,128)(2,1)S(1)} %pad_maximum_fusion.3) | copy-start | bytes 110596
  33.1 18.2 %copy-start.8 = (s32[32,6]{0,1:T(8,128)S(1)}, s32[32,6]{0,1:T(8,128)}, u32[]{:S(2)}) copy-start(s32[32,6]{0,1:T(8,128)} %param.32) | copy-start | bytes 2308
  37.1 34.2 %all-to-all-start = ((bf16[64,6,576]{2,1,0:T(8,128)(2,1)}), bf16[64,6,576]{2,1,0:T(8,128)(2,1)}, u32[]{:S(2)}, u32[]{:S(2)}) async-start(bf16[64,6,576]{2,1,0:T(8,128)(2,1)} %pad_maximum_fusion), calls=%async_computation | async-start | bytes 1310720 | tf_op jit(solution)/shard_map/all_to_all | solution.py:165
  74.2 4.3 %copy-start.13 = (s32[32]{0:T(128)}, s32[32]{0:T(128)S(1)}, u32[]{:S(2)}) copy-start(s32[32]{0:T(128)S(1)} %reduce.18) | copy-start | bytes 388
  80.8 5.4 %copy-start.7 = (s32[2496]{0:T(1024)S(1)}, s32[2496]{0:T(1024)}, u32[]{:S(2)}) copy-start(s32[2496]{0:T(1024)} %iota_add_fusion) | copy-start | bytes 29956
  80.8 5.4 %copy-start.14 = (s32[32]{0:T(128)S(1)}, s32[32]{0:T(128)}, u32[]{:S(2)}) copy-start(s32[32]{0:T(128)} %copy-done.13) | copy-start | bytes 388
  80.8 5.4 %copy-start.15 = (s32[32]{0:T(128)S(1)}, s32[32]{0:T(128)}, u32[]{:S(2)}) copy-start(s32[32]{0:T(128)} %sub.82) | copy-start | bytes 388
  81.8 14.8 %all-to-all-start.1 = ((bf16[4,32,4,576]{3,2,1,0:T(4,128)(2,1)}), bf16[4,32,4,576]{3,2,1,0:T(4,128)(2,1)}, u32[]{:S(2)}, u32[]{:S(2)}) async-start(bf16[4,32,4,576]{3,2,1,0:T(4,128)(2,1)} %stack.35), calls=%async_computation.1 | async-start | bytes 1310720 | tf_op jit(solution)/shard_map/all_to_all | solution.py:176
  116.6 6.3 %copy-start.12 = (s32[64]{0:T(128)S(1)}, s32[64]{0:T(128)}, u32[]{:S(2)}) copy-start(s32[64]{0:T(128)} %get-tuple-element.27) | copy-start | bytes 772
  117.8 13.9 %all-to-all-start.2 = ((bf16[35,16,512]{2,0,1:T(8,128)(2,1)}), bf16[35,16,512]{2,0,1:T(8,128)(2,1)}, u32[]{:S(2)}, u32[]{:S(2)}) async-start(bf16[35,16,512]{2,0,1:T(8,128)(2,1)} %copy.320), calls=%async_computation.2 | async-start | bytes 1310720 | tf_op jit(solution)/shard_map/all_to_all | solution.py:188
  123.5 9.9 %copy-start.11 = (f32[32,1,4]{0,2,1:T(4,128)S(1)}, f32[32,1,4]{0,2,1:T(4,128)}, u32[]{:S(2)}) copy-start(f32[32,1,4]{0,2,1:T(4,128)} %copy.338) | copy-start | bytes 1540
  133.1 13.6 %copy-start.10 = (s32[384]{0:T(512)S(1)}, s32[384]{0:T(512)}, u32[]{:S(2)}) copy-start(s32[384]{0:T(512)} %get-tuple-element.30) | copy-start | bytes 4612
  138.9 17.6 %all-to-all-start.3 = ((bf16[64,2,256]{2,1,0:T(2,128)(2,1)}), bf16[64,2,256]{2,1,0:T(2,128)(2,1)S(1)}, u32[]{:S(2)}, u32[]{:S(2)}) async-start(bf16[64,2,256]{2,1,0:T(2,128)(2,1)} %reshape.672), calls=%async_computation.3 | async-start | bytes 131072 | tf_op jit(solution)/shard_map/all_to_all | solution.py:217
  157.2 11.1 %copy-start.5 = (bf16[512,64]{0,1:T(8,128)(2,1)S(1)}, bf16[512,64]{0,1:T(8,128)(2,1)}, u32[]{:S(2)}) copy-start(bf16[512,64]{0,1:T(8,128)(2,1)} %param.31) | copy-start | bytes 196612
  157.2 11.0 %copy-start.9 = (f32[512]{0:T(512)S(1)}, f32[512]{0:T(512)}, u32[]{:S(2)}) copy-start(f32[512]{0:T(512)} %param.30) | copy-start | bytes 6148
  160.0 8.1 %all-to-all-start.4 = ((bf16[32,4,512]{2,0,1:T(8,128)(2,1)}), bf16[32,4,512]{2,0,1:T(8,128)(2,1)S(1)}, u32[]{:S(2)}, u32[]{:S(2)}) async-start(bf16[32,4,512]{2,0,1:T(8,128)(2,1)} %bitcast.128), calls=%async_computation.4 | async-start | bytes 262144 | tf_op jit(solution)/shard_map/all_to_all | solution.py:54
  168.3 12.4 %copy-start.3 = (bf16[32,512]{1,0:T(8,128)(2,1)}, bf16[32,512]{1,0:T(8,128)(2,1)S(1)}, u32[]{:S(2)}) copy-start(bf16[32,512]{1,0:T(8,128)(2,1)S(1)} %get-tuple-element.38) | copy-start | bytes 98308
  215.9 24.2 %copy-start.17 = (bf16[1,2048,352]{1,2,0:T(8,128)(2,1)S(1)}, bf16[1,2048,352]{1,2,0:T(8,128)(2,1)}, u32[]{:S(2)}) copy-start(bf16[1,2048,352]{1,2,0:T(8,128)(2,1)} %param.33) | copy-start | bytes 4325380
  239.0 1.1 copy-start.2
  250.0 4.5 %copy-start.6 = (s32[32,6]{1,0:T(8,128)S(1)}, s32[32,6]{1,0:T(8,128)}, u32[]{:S(2)}) copy-start(s32[32,6]{1,0:T(8,128)} %get-tuple-element.35) | copy-start | bytes 2308
  250.0 24.1 %all-to-all-start.7 = ((bf16[384,4,512]{2,0,1:T(8,128)(2,1)}), bf16[384,4,512]{2,0,1:T(8,128)(2,1)}, u32[]{:S(2)}, u32[]{:S(2)}) async-start(bf16[384,4,512]{2,0,1:T(8,128)(2,1)} %bitcast.132), calls=%async_computation.7 | async-start | bytes 3145728 | tf_op jit(solution)/shard_map/all_to_all | solution.py:54
  276.8 25.3 %all-to-all-start.8 = ((bf16[64,6,512]{2,1,0:T(8,128)(2,1)}), bf16[64,6,512]{2,1,0:T(8,128)(2,1)}, u32[]{:S(2)}, u32[]{:S(2)}) async-start(bf16[64,6,512]{2,1,0:T(8,128)(2,1)} %reshape.559), calls=%async_computation.8 | async-start | bytes 1048576 | tf_op jit(solution)/shard_map/all_to_all | solution.py:279
